TPU v7x, 128 devices: a whole 4x4x4 slice. The times are simulated.
128 devices in a mesh: shard: 8 (over x, core), tensor: 16 (over z, y).
Axes of the slice: x: 4, y: 4, z: 4, core: 2. Of those that a mesh axis runs over, the one named last changes fastest.
Arguments:
- grad_square: bfloat16 [8, 768, 768], P(None, 'shard'), may hold values from -64 to 64
- grad_wide: bfloat16 [8, 2048, 768], P(None, 'shard'), may hold values from -64 to 64
- moment_square: float32 [8, 589824], P(None, ('shard', 'tensor')), may hold values from -6 to 6
- moment_wide: float32 [8, 1572864], P(None, ('shard', 'tensor')), may hold values from -6 to 6
Outputs:
- update_square: float32 [8, 768, 768], P(None, 'shard')
- update_wide: float32 [8, 2048, 768], P(None, 'shard')
- new_moment_square: float32 [8, 589824], P(None, ('shard', 'tensor'))
- new_moment_wide: float32 [8, 1572864], P(None, ('shard', 'tensor'))
All inputs are finite; a program needn't handle non-finite values.
Results may differ from a plain program's by a relative error of at most 0.0003.
Values sent between devices are 32-bit elements; how exact they have to be, the bound alone decides.
No kernel may reach another device: no remote copies, remote signals or barrier semaphores. Data moves between devices by JAX's collectives and lax.ppermute only.
A program may use at most 128 MiB of HBM per device.

v0:
```python
import math
import jax
import jax.numpy as jnp
from jax import lax
from jax.sharding import PartitionSpec as P

D = 768
FF = 2048
ITERS = 3
coef_a = 3.4445
coef_b = -4.775
coef_c = 2.0315
momentum_decay = 0.95
epsilon = 1e-07


def polynomial(row_gram, whole_gram):
    square_part = jnp.einsum(
        "mcd,mde->mce",
        row_gram,
        whole_gram,
        precision=lax.Precision.HIGHEST,
        preferred_element_type=jnp.float32,
    )
    return coef_b * row_gram + coef_c * square_part


def next_iterate(current, mixer):
    product = jnp.einsum(
        "mrc,mcd->mrd",
        current,
        mixer,
        precision=lax.Precision.HIGHEST,
        preferred_element_type=jnp.float32,
    )
    return coef_a * current + product


def partial_gram(current):
    return jnp.einsum(
        "mrc,mrd->mcd",
        current,
        current,
        precision=lax.Precision.HIGHEST,
        preferred_element_type=jnp.float32,
    )


def squares(values):
    return jnp.sum(values * values, axis=(1, 2))


def normalize(values, totals):
    return values / (jnp.sqrt(totals) + epsilon)[:, None, None]


def own_rows(grad, member, tensor_count):
    row_piece = grad.shape[1] // tensor_count
    return lax.dynamic_slice_in_dim(grad, member * row_piece, row_piece, 1)


def shards(grad_square, grad_wide, moment_square, moment_wide):
    tensor_count = lax.axis_size("tensor")
    member = lax.axis_index("tensor")
    flat_square = own_rows(grad_square, member, tensor_count).astype(jnp.float32)
    flat_wide = own_rows(grad_wide, member, tensor_count).astype(jnp.float32)
    new_square = momentum_decay * moment_square.reshape(flat_square.shape) + flat_square
    new_wide = momentum_decay * moment_wide.reshape(flat_wide.shape) + flat_wide
    look_square = flat_square + momentum_decay * new_square
    look_wide = flat_wide + momentum_decay * new_wide
    total_square, total_wide = lax.psum(
        (squares(look_square), squares(look_wide)), ("shard", "tensor")
    )
    start_square = normalize(look_square, total_square)
    start_wide = normalize(look_wide, total_wide)
    held_square, held_wide = (
        lax.all_to_all(start_square, "shard", split_axis=0, concat_axis=1, tiled=True),
        lax.all_to_all(start_wide, "shard", split_axis=0, concat_axis=1, tiled=True),
    )
    for iteration in range(ITERS):
        part_square = partial_gram(held_square)
        part_wide = partial_gram(held_wide)
        gram_square, gram_wide = lax.psum((part_square, part_wide), "tensor")
        mixer_square = polynomial(gram_square, gram_square)
        mixer_wide = polynomial(gram_wide, gram_wide)
        held_square = next_iterate(held_square, mixer_square)
        held_wide = next_iterate(held_wide, mixer_wide)
    scaled_square = math.sqrt(D) * held_square
    scaled_wide = math.sqrt(FF) * held_wide
    back_square, back_wide = (
        lax.all_to_all(scaled_square, "shard", split_axis=1, concat_axis=0, tiled=True),
        lax.all_to_all(scaled_wide, "shard", split_axis=1, concat_axis=0, tiled=True),
    )
    update_square, update_wide = (
        lax.all_gather(back_square, "tensor", axis=1, tiled=True),
        lax.all_gather(back_wide, "tensor", axis=1, tiled=True),
    )
    return (
        update_square,
        update_wide,
        new_square.reshape(moment_square.shape),
        new_wide.reshape(moment_wide.shape),
    )


def solution(mesh):
    return jax.shard_map(
        shards,
        mesh=mesh,
        in_specs=(
            P(None, "shard", None),
            P(None, "shard", None),
            P(None, ("shard", "tensor")),
            P(None, ("shard", "tensor")),
        ),
        out_specs=(
            P(None, "shard", None),
            P(None, "shard", None),
            P(None, ("shard", "tensor")),
            P(None, ("shard", "tensor")),
        ),
        check_vma=False,
    )
```

profile of v0, /device:TPU:1, one launch (start us, length us, event | category | flops | bytes accessed | tf_op | source)
XLA Modules:
  0.0 619.9 jit_solution(17534331259739057778)
XLA Ops:
  11.3 68.6 %all-reduce = (f32[8]{0:T(128)S(1)}, f32[8]{0:T(128)S(1)}) all-reduce(f32[8]{0:T(128)S(1)} %get-tuple-element.23, f32[8]{0:T(128)S(1)} %multiply_reduce_fusion), channel_id=1, replica_groups=mesh['shard'=8,'tensor'=16] {'shard','tensor'}, use_global_device_ids=true, to_apply=%region_1.0 | all-reduce | flops 16 | bytes 128 | tf_op jit(solution)/shard_map/psum | solution.py:71
  80.7 4.2 all-to-all-start
  86.9 3.9 all-to-all-done
  90.8 4.3 all-to-all-start.2
  95.1 3.5 convolution_bitcast_fusion
  98.6 4.3 all-to-all-done.2
  106.6 105.0 %all-reduce.12.cloned.1.call-done = (f32[1,768,768]{2,1,0:T(8,128)}, f32[1,768,768]{2,1,0:T(8,128)}) async-done(((f32[1,768,768]{2,1,0:T(8,128)}, f32[1,768,768]{2,1,0:T(8,128)}), (f32[1,768,768]{2,1,0:T(8,128)}, f32[1,768,768]{2,1,0:T(8,128)})) %all-reduce.12.cloned.1.call-update) | async-done | bytes 4718608 | tf_op jit(solution)/shard_map/psum | solution.py:83
  211.6 8.5 %fusion.22 = f32[768,768]{1,0:T(8,128)S(1)} fusion(f32[1,768,768]{2,1,0:T(8,128)} %get-tuple-element.18), kind=kOutput, calls=%fused_computation.28 | convolution fusion | flops 5435817984 | bytes 4718592 | tf_op jit(solution)/shard_map/mcd,mde->mce/dot_general | solution.py:18
  221.9 3.5 convolution_bitcast_fusion.5
  225.4 6.4 %fusion.10 = f32[768,768]{1,0:T(8,128)S(1)} fusion(f32[1,768,768]{2,1,0:T(8,128)S(1)} %copy-done.6), kind=kOutput, calls=%fused_computation.13 | convolution fusion | flops 5435817984 | bytes 4718592 | tf_op jit(solution)/shard_map/mcd,mde->mce/dot_general | solution.py:18
  237.0 108.1 %all-reduce.10.cloned.1.call-done = (f32[1,768,768]{2,1,0:T(8,128)}, f32[1,768,768]{2,1,0:T(8,128)}) async-done(((f32[1,768,768]{2,1,0:T(8,128)}, f32[1,768,768]{2,1,0:T(8,128)}), (f32[1,768,768]{2,1,0:T(8,128)}, f32[1,768,768]{2,1,0:T(8,128)})) %all-reduce.10.cloned.1.call-update) | async-done | bytes 4718608 | tf_op jit(solution)/shard_map/psum | solution.py:83
  345.1 8.5 %fusion.18 = f32[768,768]{1,0:T(8,128)S(1)} fusion(f32[1,768,768]{2,1,0:T(8,128)} %get-tuple-element.16), kind=kOutput, calls=%fused_computation.23 | convolution fusion | flops 5435817984 | bytes 4718592 | tf_op jit(solution)/shard_map/mcd,mde->mce/dot_general | solution.py:18
  355.4 3.5 convolution_bitcast_fusion.4
  358.8 6.1 fusion.6
  366.7 3.5 convolution_bitcast_fusion.1
  370.2 108.1 %all-reduce.8.cloned.1.call-done = (f32[1,768,768]{2,1,0:T(8,128)}, f32[1,768,768]{2,1,0:T(8,128)}) async-done(((f32[1,768,768]{2,1,0:T(8,128)}, f32[1,768,768]{2,1,0:T(8,128)}), (f32[1,768,768]{2,1,0:T(8,128)}, f32[1,768,768]{2,1,0:T(8,128)})) %all-reduce.8.cloned.1.call-update) | async-done | bytes 4718608 | tf_op jit(solution)/shard_map/psum | solution.py:83
  478.3 8.5 %fusion.14 = f32[768,768]{1,0:T(8,128)S(1)} fusion(f32[1,768,768]{2,1,0:T(8,128)} %get-tuple-element.14), kind=kOutput, calls=%fused_computation.18 | convolution fusion | flops 5435817984 | bytes 4718592 | tf_op jit(solution)/shard_map/mcd,mde->mce/dot_general | solution.py:18
  488.8 10.3 %all_to_all.48 = f32[1,48,768]{2,0,1:T(1,128)S(1)} all-to-all(f32[1,48,768]{2,0,1:T(1,128)S(1)} %copy.19), channel_id=1, replica_groups=mesh['shard'=8,'tensor'=16] {'shard'}, dimensions={1} | all-to-all | bytes 294912 | tf_op jit(solution)/shard_map/all_to_all | solution.py:91
  500.5 6.0 fusion.2
  508.6 11.3 %all_to_all.49 = f32[1,128,768]{2,0,1:T(1,128)S(1)} all-to-all(f32[1,128,768]{2,0,1:T(1,128)S(1)} %copy.21), channel_id=1, replica_groups=mesh['shard'=8,'tensor'=16] {'shard'}, dimensions={1} | all-to-all | bytes 786432 | tf_op jit(solution)/shard_map/all_to_all | solution.py:92
  521.7 21.0 %all-gather.3.cloned.1.call-done = f32[8,96,768]{2,0,1:T(8,128)} async-done(((f32[8,6,768]{2,0,1:T(8,128)}), f32[8,96,768]{2,0,1:T(8,128)}) %all-gather.3.cloned.1.call-update) | async-done | bytes 2359312 | tf_op jit(solution)/shard_map/all_gather | solution.py:95
  542.7 3.8 copy.22
  546.5 60.6 %all-gather.5.cloned.1.call-done = f32[8,256,768]{2,1,0:T(8,128)} async-done(((f32[8,16,768]{2,1,0:T(8,128)}), f32[8,256,768]{2,1,0:T(8,128)}) %all-gather.5.cloned.1.call-update) | async-done | bytes 6291472 | tf_op jit(solution)/shard_map/all_gather | solution.py:96
  607.1 6.0 copy.51
  (53 shorter events, 28.3 us)
Async XLA Ops:
  7.2 2.1 copy-start
  80.7 10.1 %all-to-all-start = ((f32[8,6,768]{2,1,0:T(8,128)}), f32[8,6,768]{2,1,0:T(8,128)S(1)}, u32[]{:S(2)}, u32[]{:S(2)}) async-start(f32[8,6,768]{2,1,0:T(8,128)} %copy.18), calls=%async_computation | async-start | bytes 393216 | tf_op jit(solution)/shard_map/all_to_all | solution.py:77
  90.8 12.0 %all-to-all-start.2 = ((f32[8,16,768]{2,1,0:T(8,128)}), f32[8,16,768]{2,1,0:T(8,128)S(1)}, u32[]{:S(2)}, u32[]{:S(2)}) async-start(f32[8,16,768]{2,1,0:T(8,128)} %get-tuple-element.21), calls=%async_computation.2 | async-start | bytes 786432 | tf_op jit(solution)/shard_map/all_to_all | solution.py:78
  95.1 116.4 %all-reduce.12.cloned.1.call-start = ((), (), s32[]{:S(2)}) async-start(), calls=%async_computation.8 | async-start | bytes 9437184 | tf_op jit(solution)/shard_map/psum | solution.py:83
  106.3 238.7 %all-reduce.10.cloned.1.call-start = ((), (), s32[]{:S(2)}) async-start(), calls=%async_computation.7 | async-start | bytes 9437184 | tf_op jit(solution)/shard_map/psum | solution.py:83
  211.6 8.5 %copy-start.2 = (f32[1,768,768]{2,1,0:T(8,128)S(1)}, f32[1,768,768]{2,1,0:T(8,128)}, u32[]{:S(2)}) copy-start(f32[1,768,768]{2,1,0:T(8,128)} %get-tuple-element.18) | copy-start | bytes 7077892
  221.9 3.5 copy-start.6
  236.9 241.4 %all-reduce.8.cloned.1.call-start = ((), (), s32[]{:S(2)}) async-start(), calls=%async_computation.6 | async-start | bytes 9437184 | tf_op jit(solution)/shard_map/psum | solution.py:83
  345.1 8.5 %copy-start.3 = (f32[1,768,768]{2,1,0:T(8,128)S(1)}, f32[1,768,768]{2,1,0:T(8,128)}, u32[]{:S(2)}) copy-start(f32[1,768,768]{2,1,0:T(8,128)} %get-tuple-element.16) | copy-start | bytes 7077892
  355.4 3.5 copy-start.7
  370.2 172.5 %all-gather.3.cloned.1.call-start = ((), (), s32[]{:S(2)}) async-start(), calls=%async_computation.4 | async-start | bytes 2506752 | tf_op jit(solution)/shard_map/all_gather | solution.py:95
  478.3 8.5 %copy-start.4 = (f32[1,768,768]{2,1,0:T(8,128)S(1)}, f32[1,768,768]{2,1,0:T(8,128)}, u32[]{:S(2)}) copy-start(f32[1,768,768]{2,1,0:T(8,128)} %get-tuple-element.14) | copy-start | bytes 7077892
  486.9 13.6 %copy-start.5 = (f32[1,768,768]{2,1,0:T(8,128)S(1)}, f32[1,768,768]{2,1,0:T(8,128)}, u32[]{:S(2)}) copy-start(f32[1,768,768]{2,1,0:T(8,128)} %get-tuple-element.15) | copy-start | bytes 7077892
  500.2 106.9 %all-gather.5.cloned.1.call-start = ((), (), s32[]{:S(2)}) async-start(), calls=%async_computation.5 | async-start | bytes 6684672 | tf_op jit(solution)/shard_map/all_gather | solution.py:96
  508.2 12.5 %copy-start.8 = (f32[1,8,16,768]{3,2,1,0:T(8,128)S(1)}, f32[1,8,16,768]{3,2,1,0:T(8,128)}, u32[]{:S(2)}) copy-start(f32[1,8,16,768]{3,2,1,0:T(8,128)} %get-tuple-element.20) | copy-start | bytes 1179652
  607.1 6.0 copy-start.1
Sparse Core Ops, SparseCore 0:
  106.5 105.0 all-reduce.11
  237.0 107.9 all-reduce.9
  370.3 107.9 all-reduce.7
  500.3 42.3 all-gather.2
  545.3 61.8 all-gather.4
where the time goes:
time: 625 us; the launch traced here: 620 us
  waiting for transfers between devices  411 us (66%)
  blocking collectives  90.2 us (14%)
  matrix products  75.2 us (12%)
  between operations  14.3 us (2%)
  local copies, waits for them, and re-layouts  13.7 us (2%)
  starting transfers between devices  9.07 us (1%)
  other arithmetic  6.42 us (1%)
    psum x3, waiting for transfers between devices, shards(): gram_square, gram_wide = lax.psum((part_square, part_wide), 'tensor')  321 us
    psum x1, blocking collectives, shards(): lax.psum((squares(look_square), squares(look_wide)), ('shard', 'tensor'))  68.6 us
    all_gather x1, waiting for transfers between devices, shards(): lax.all_gather(back_wide, 'tensor', axis=1, tiled=True)  60.6 us
    dot_general x6, matrix products, polynomial(): jnp.einsum('mcd,mde->mce', row_gram, whole_gram, precision=lax.Precision....  44 us
    all_gather x1, waiting for transfers between devices, shards(): lax.all_gather(back_square, 'tensor', axis=1, tiled=True)  21 us
    dot_general x6, matrix products, partial_gram(): jnp.einsum('mrc,mrd->mcd', current, current, precision=lax.Precision.HIGH...  20.8 us
  transfers between devices with their start and end apart: 7, of which 7 were waited for; matrix products, arithmetic and copies ran while one was open for 3% of the time, Pallas kernels for 0%

commit v1 on v0

--- a/solution.py
+++ b/solution.py
@@ -92,7 +92,10 @@
         lax.all_to_all(scaled_wide, "shard", split_axis=1, concat_axis=0, tiled=True),
     )
     update_square, update_wide = (
-        lax.all_gather(back_square, "tensor", axis=1, tiled=True),
+        jnp.concatenate(
+            lax.all_to_all(jnp.stack([back_square] * lax.axis_size("tensor")), "tensor", 0, 0),
+            axis=1,
+        ),
         lax.all_gather(back_wide, "tensor", axis=1, tiled=True),
     )
     return (

time: 625 us -> 600 us (0.960)
  waiting for transfers between devices: 411 us -> 381 us
    all_gather x1, waiting for transfers between devices: 60.6 us -> 7.85 us  [shards(): lax.all_gather(back_wide, 'tensor', axis=1, tiled=True)]
    all_to_all x0 -> x1, waiting for transfers between devices: none -> 44 us  [shards(): lax.all_to_all(jnp.stack([back_square] * lax.axis_size('tensor')), 'tenso...]
    all_gather x1 -> x0, waiting for transfers between devices: 21 us -> none  [shards(): lax.all_gather(back_square, 'tensor', axis=1, tiled=True)]
where the time goes in v1:
time: 600 us; the launch traced here: 595 us
  waiting for transfers between devices  381 us (64%)
  blocking collectives  90.6 us (15%)
  matrix products  75.2 us (13%)
  between operations  14.2 us (2%)
  starting transfers between devices  14 us (2%)
  local copies, waits for them, and re-layouts  13 us (2%)
  other arithmetic  6.42 us (1%)
    psum x3, waiting for transfers between devices, shards(): gram_square, gram_wide = lax.psum((part_square, part_wide), 'tensor')  321 us
    psum x1, blocking collectives, shards(): lax.psum((squares(look_square), squares(look_wide)), ('shard', 'tensor'))  68.6 us
    all_to_all x1, waiting for transfers between devices, shards(): lax.all_to_all(jnp.stack([back_square] * lax.axis_size('tensor')), 'tenso...  44 us
    dot_general x6, matrix products, polynomial(): jnp.einsum('mcd,mde->mce', row_gram, whole_gram, precision=lax.Precision....  44 us
    dot_general x6, matrix products, partial_gram(): jnp.einsum('mrc,mrd->mcd', current, current, precision=lax.Precision.HIGH...  20.8 us
    all_to_all x1, blocking collectives, shards(): lax.all_to_all(scaled_wide, 'shard', split_axis=1, concat_axis=0, tiled=T...  13.3 us
  transfers between devices with their start and end apart: 7, of which 7 were waited for; matrix products, arithmetic and copies ran while one was open for 3% of the time, Pallas kernels for 0%

profile of v1, /device:TPU:1, one launch (start us, length us, event | category | flops | bytes accessed | tf_op | source)
XLA Modules:
  0.0 594.7 jit_solution(5053911821625027159)
XLA Ops:
  11.3 68.6 %all-reduce = (f32[8]{0:T(128)S(1)}, f32[8]{0:T(128)S(1)}) all-reduce(f32[8]{0:T(128)S(1)} %get-tuple-element.27, f32[8]{0:T(128)S(1)} %multiply_reduce_fusion), channel_id=1, replica_groups=mesh['shard'=8,'tensor'=16] {'shard','tensor'}, use_global_device_ids=true, to_apply=%region_1.0 | all-reduce | flops 16 | bytes 128 | tf_op jit(solution)/shard_map/psum | solution.py:71
  80.7 4.2 all-to-all-start
  86.9 3.9 all-to-all-done
  90.8 4.3 all-to-all-start.3
  95.1 3.5 convolution_bitcast_fusion
  98.6 4.2 all-to-all-done.3
  106.6 105.0 %all-reduce.12.cloned.1.call-done = (f32[1,768,768]{2,1,0:T(8,128)}, f32[1,768,768]{2,1,0:T(8,128)}) async-done(((f32[1,768,768]{2,1,0:T(8,128)}, f32[1,768,768]{2,1,0:T(8,128)}), (f32[1,768,768]{2,1,0:T(8,128)}, f32[1,768,768]{2,1,0:T(8,128)})) %all-reduce.12.cloned.1.call-update) | async-done | bytes 4718608 | tf_op jit(solution)/shard_map/psum | solution.py:83
  211.6 8.5 %fusion.22 = f32[768,768]{1,0:T(8,128)S(1)} fusion(f32[1,768,768]{2,1,0:T(8,128)} %get-tuple-element.22), kind=kOutput, calls=%fused_computation.28 | convolution fusion | flops 5435817984 | bytes 4718592 | tf_op jit(solution)/shard_map/mcd,mde->mce/dot_general | solution.py:18
  221.9 3.5 convolution_bitcast_fusion.5
  225.3 6.4 %fusion.10 = f32[768,768]{1,0:T(8,128)S(1)} fusion(f32[1,768,768]{2,1,0:T(8,128)S(1)} %copy-done.5), kind=kOutput, calls=%fused_computation.13 | convolution fusion | flops 5435817984 | bytes 4718592 | tf_op jit(solution)/shard_map/mcd,mde->mce/dot_general | solution.py:18
  233.4 3.5 convolution_bitcast_fusion.2
  237.0 108.1 %all-reduce.10.cloned.1.call-done = (f32[1,768,768]{2,1,0:T(8,128)}, f32[1,768,768]{2,1,0:T(8,128)}) async-done(((f32[1,768,768]{2,1,0:T(8,128)}, f32[1,768,768]{2,1,0:T(8,128)}), (f32[1,768,768]{2,1,0:T(8,128)}, f32[1,768,768]{2,1,0:T(8,128)})) %all-reduce.10.cloned.1.call-update) | async-done | bytes 4718608 | tf_op jit(solution)/shard_map/psum | solution.py:83
  345.0 8.5 %fusion.18 = f32[768,768]{1,0:T(8,128)S(1)} fusion(f32[1,768,768]{2,1,0:T(8,128)} %get-tuple-element.20), kind=kOutput, calls=%fused_computation.23 | convolution fusion | flops 5435817984 | bytes 4718592 | tf_op jit(solution)/shard_map/mcd,mde->mce/dot_general | solution.py:18
  355.4 3.5 convolution_bitcast_fusion.4
  358.8 6.2 %fusion.6 = f32[768,768]{1,0:T(8,128)S(1)} fusion(f32[1,768,768]{2,1,0:T(8,128)S(1)} %copy-done.6), kind=kOutput, calls=%fused_computation.8 | convolution fusion | flops 5435817984 | bytes 4718592 | tf_op jit(solution)/shard_map/mcd,mde->mce/dot_general | solution.py:18
  370.2 108.1 %all-reduce.8.cloned.1.call-done = (f32[1,768,768]{2,1,0:T(8,128)}, f32[1,768,768]{2,1,0:T(8,128)}) async-done(((f32[1,768,768]{2,1,0:T(8,128)}, f32[1,768,768]{2,1,0:T(8,128)}), (f32[1,768,768]{2,1,0:T(8,128)}, f32[1,768,768]{2,1,0:T(8,128)})) %all-reduce.8.cloned.1.call-update) | async-done | bytes 4718608 | tf_op jit(solution)/shard_map/psum | solution.py:83
  478.3 8.5 %fusion.2 = f32[768,768]{1,0:T(8,128)S(1)} fusion(f32[1,768,768]{2,1,0:T(8,128)} %get-tuple-element.19), kind=kOutput, calls=%fused_computation.3 | convolution fusion | flops 5435817984 | bytes 4718592 | tf_op jit(solution)/shard_map/mcd,mde->mce/dot_general | solution.py:18
  488.9 13.3 %all_to_all.50 = f32[1,128,768]{2,0,1:T(1,128)S(1)} all-to-all(f32[1,128,768]{2,0,1:T(1,128)S(1)} %copy.23), channel_id=1, replica_groups=mesh['shard'=8,'tensor'=16] {'shard'}, dimensions={1} | all-to-all | bytes 786432 | tf_op jit(solution)/shard_map/all_to_all | solution.py:92
  503.0 6.0 %fusion.14 = f32[768,768]{1,0:T(8,128)S(1)} fusion(f32[1,768,768]{2,1,0:T(8,128)S(1)} %copy-done.2), kind=kOutput, calls=%fused_computation.18 | convolution fusion | flops 5435817984 | bytes 4718592 | tf_op jit(solution)/shard_map/mcd,mde->mce/dot_general | solution.py:18
  511.0 8.6 %all_to_all.51 = f32[1,48,768]{2,0,1:T(1,128)S(1)} all-to-all(f32[1,48,768]{2,0,1:T(1,128)S(1)} %copy.21), channel_id=1, replica_groups=mesh['shard'=8,'tensor'=16] {'shard'}, dimensions={1} | all-to-all | bytes 294912 | tf_op jit(solution)/shard_map/all_to_all | solution.py:91
  521.7 5.2 all-to-all-start.2
  527.9 44.0 %all-to-all-done.2 = f32[16,8,6,768]{3,1,2,0:T(8,128)S(1)} async-done(((f32[16,8,6,768]{3,1,2,0:T(8,128)}), f32[16,8,6,768]{3,1,2,0:T(8,128)S(1)}, u32[]{:S(2)}, u32[]{:S(2)}) %all-to-all-start.2) | async-done | bytes 2359328 | tf_op jit(solution)/shard_map/all_to_all | solution.py:96
  574.1 7.8 %all-gather.2.cloned.1.call-done = f32[8,256,768]{2,1,0:T(8,128)} async-done(((f32[8,16,768]{2,1,0:T(8,128)}), f32[8,256,768]{2,1,0:T(8,128)}) %all-gather.2.cloned.1.call-update) | async-done | bytes 6291472 | tf_op jit(solution)/shard_map/all_gather | solution.py:99
  581.9 6.0 %copy.53 = f32[8,256,768]{2,1,0:T(8,128)} copy(f32[8,256,768]{2,1,0:T(8,128)} %all-gather.2.cloned.1.call-done) | data formatting | bytes 12582912
  (53 shorter events, 31.1 us)
Async XLA Ops:
  7.2 2.1 copy-start
  80.7 10.1 %all-to-all-start = ((f32[8,6,768]{2,1,0:T(8,128)}), f32[8,6,768]{2,1,0:T(8,128)S(1)}, u32[]{:S(2)}, u32[]{:S(2)}) async-start(f32[8,6,768]{2,1,0:T(8,128)} %copy.20), calls=%async_computation | async-start | bytes 393216 | tf_op jit(solution)/shard_map/all_to_all | solution.py:77
  90.8 12.0 %all-to-all-start.3 = ((f32[8,16,768]{2,1,0:T(8,128)}), f32[8,16,768]{2,1,0:T(8,128)S(1)}, u32[]{:S(2)}, u32[]{:S(2)}) async-start(f32[8,16,768]{2,1,0:T(8,128)} %get-tuple-element.25), calls=%async_computation.3 | async-start | bytes 786432 | tf_op jit(solution)/shard_map/all_to_all | solution.py:78
  95.1 116.4 %all-reduce.12.cloned.1.call-start = ((), (), s32[]{:S(2)}) async-start(), calls=%async_computation.8 | async-start | bytes 9437184 | tf_op jit(solution)/shard_map/psum | solution.py:83
  106.3 238.7 %all-reduce.10.cloned.1.call-start = ((), (), s32[]{:S(2)}) async-start(), calls=%async_computation.7 | async-start | bytes 9437184 | tf_op jit(solution)/shard_map/psum | solution.py:83
  211.6 8.5 %copy-start.3 = (f32[1,768,768]{2,1,0:T(8,128)S(1)}, f32[1,768,768]{2,1,0:T(8,128)}, u32[]{:S(2)}) copy-start(f32[1,768,768]{2,1,0:T(8,128)} %get-tuple-element.22) | copy-start | bytes 7077892
  221.9 3.5 copy-start.5
  236.9 241.4 %all-reduce.8.cloned.1.call-start = ((), (), s32[]{:S(2)}) async-start(), calls=%async_computation.6 | async-start | bytes 9437184 | tf_op jit(solution)/shard_map/psum | solution.py:83
  345.0 8.5 %copy-start.4 = (f32[1,768,768]{2,1,0:T(8,128)S(1)}, f32[1,768,768]{2,1,0:T(8,128)}, u32[]{:S(2)}) copy-start(f32[1,768,768]{2,1,0:T(8,128)} %get-tuple-element.20) | copy-start | bytes 7077892
  355.3 3.5 copy-start.6
  370.1 211.8 %all-gather.2.cloned.1.call-start = ((), (), s32[]{:S(2)}) async-start(), calls=%async_computation.5 | async-start | bytes 6684672 | tf_op jit(solution)/shard_map/all_gather | solution.py:99
  478.3 8.5 %copy-start.7 = (f32[1,768,768]{2,1,0:T(8,128)S(1)}, f32[1,768,768]{2,1,0:T(8,128)}, u32[]{:S(2)}) copy-start(f32[1,768,768]{2,1,0:T(8,128)} %get-tuple-element.19) | copy-start | bytes 7077892
  488.5 14.5 %copy-start.2 = (f32[1,768,768]{2,1,0:T(8,128)S(1)}, f32[1,768,768]{2,1,0:T(8,128)}, u32[]{:S(2)}) copy-start(f32[1,768,768]{2,1,0:T(8,128)} %get-tuple-element.18) | copy-start | bytes 7077892
  521.7 5.2 copy-start.8
  521.7 50.2 %all-to-all-start.2 = ((f32[16,8,6,768]{3,1,2,0:T(8,128)}), f32[16,8,6,768]{3,1,2,0:T(8,128)S(1)}, u32[]{:S(2)}, u32[]{:S(2)}) async-start(f32[16,8,6,768]{3,1,2,0:T(8,128)} %stack.5), calls=%async_computation.2 | async-start | bytes 4718592 | tf_op jit(solution)/shard_map/all_to_all | solution.py:96
  581.9 6.0 %copy-start.1 = (bf16[8,96,768]{2,1,0:T(8,128)(2,1)S(1)}, bf16[8,96,768]{2,1,0:T(8,128)(2,1)}, u32[]{:S(2)}) copy-start(bf16[8,96,768]{2,1,0:T(8,128)(2,1)} %param.4) | copy-start | bytes 3538948
Sparse Core Ops, SparseCore 0:
  106.5 105.0 all-reduce.11
  237.0 107.9 all-reduce.9
  370.3 107.9 all-reduce.7
  503.1 78.7 all-gather.1
